TPU v7x, 256 devices: a whole 4x4x8 slice. The times are simulated.
256 devices in a mesh: depth: 8 (over y_hi, x), shots: 32 (over z, y_lo, core).
Axes of the slice: x: 4, y: 4 (y_hi: 2, y_lo: 2; y = y_hi * 2 + y_lo), z: 8, core: 2. Of those that a mesh axis runs over, the one named last changes fastest.
Arguments:
- adj_now: float32 [32, 128, 128, 128], P('shots', 'depth'), may hold values from -6 to 6
- adj_prev: float32 [32, 128, 128, 128], P('shots', 'depth'), may hold values from -6 to 6
- fwd_snap: bfloat16 [32, 4, 128, 128, 128], P('shots', None, 'depth'), may hold values from -6 to 6
- velocity: float32 [128, 128, 128], P('depth', 'shots'), may hold values from 1 to 2
- density: float32 [128, 128, 128], P('depth', 'shots'), may hold values from 1 to 2
- shot_count: int32 [32], P('shots'), may hold values from 1 to 12, 128 in all
- rec_x: int32 [32, 256], P('shots'), may hold values from 0 to 127
- rec_y: int32 [32, 256], P('shots'), may hold values from 0 to 127
- residual: float32 [32, 4, 256], P('shots'), may hold values from -6 to 6
Outputs:
- out_now: float32 [32, 128, 128, 128], P('shots', 'depth')
- out_prev: float32 [32, 128, 128, 128], P('shots', 'depth')
- grad_vel: float32 [128, 128, 128], P('depth', 'shots')
Inputs may be any that keep to these rules, and one draw needn't show every extreme that they name: `shot_count`: the counts sum to 128; the largest is exactly 12.
All inputs are finite; a program needn't handle non-finite values.
Results may differ from a plain program's by a relative error of at most 0.0003.
Values sent between devices are 32-bit elements; how exact they have to be, the bound alone decides.
No kernel may reach another device: no remote copies, remote signals or barrier semaphores. Data moves between devices by JAX's collectives and lax.ppermute only.
A program may use at most 64 MiB of HBM per device.

v0:
```python
import jax
import jax.numpy as jnp
from jax import lax
from jax.sharding import PartitionSpec as P


def with_halo(shard, sides, width):
    for axis, dim in sides:
        peers, length = (lax.axis_size(axis), shard.shape[dim])
        up = [(i, (i + 1) % peers) for i in range(peers - 1)]
        down = [(j, i) for i, j in up]
        last = lax.slice_in_dim(shard, length - width, length, axis=dim)
        first = lax.slice_in_dim(shard, 0, width, axis=dim)
        before = lax.ppermute(last, axis, up)
        after = lax.ppermute(first, axis, down)
        shard = jnp.concatenate([before, shard, after], axis=dim)
    return shard


def operate(field, buoy):
    padded = jnp.pad(field, 1)
    bpad = jnp.pad(buoy, 1)
    total = jnp.zeros_like(field)
    for axis in range(3):
        center = [slice(1, -1)] * 3
        ahead = list(center)
        behind = list(center)
        ahead[axis] = slice(2, None)
        behind[axis] = slice(0, -2)
        pc, pa, pb = (padded[tuple(center)], padded[tuple(ahead)], padded[tuple(behind)])
        bc, ba, bb = (bpad[tuple(center)], bpad[tuple(ahead)], bpad[tuple(behind)])
        total = total + 0.5 * (bc + ba) * (pa - pc) - 0.5 * (bb + bc) * (pc - pb)
    return total


def source_plane(rows_x, rows_y, amounts, width_x, width_y):
    onehot_x = (rows_x[:, None] == jnp.arange(width_x, dtype=jnp.int32)[None, :]).astype(
        jnp.float32
    )
    onehot_y = (rows_y[:, None] == jnp.arange(width_y, dtype=jnp.int32)[None, :]).astype(
        jnp.float32
    )
    return jnp.dot((onehot_x * amounts[:, None]).T, onehot_y, precision=lax.Precision.HIGHEST)


def body(adj_now, adj_prev, fwd_snap, velocity, density, shot_count, rec_x, rec_y, residual):
    depth_planes = adj_now.shape[1]
    width_x = adj_now.shape[2]
    width_y = adj_now.shape[3]
    steps = fwd_snap.shape[1]
    groups = lax.axis_size("shots")
    width = 1
    vel_all, rho_all = (
        lax.all_gather(velocity, "shots", axis=1, tiled=True),
        lax.all_gather(density, "shots", axis=1, tiled=True),
    )
    packed = jnp.stack([rho_all * vel_all * vel_all, 1.0 / rho_all])
    extended = with_halo(packed, (("depth", 1),), width)
    buoy_ext = extended[1]
    first = lax.axis_index("depth") * depth_planes
    snaps = fwd_snap[0]
    rows_x = rec_x[0]
    rows_y = rec_y[0]
    image = jnp.zeros((depth_planes, width_x, width_y), jnp.float32)
    kappa_ext = extended[0, width : width + depth_planes]
    global_plane = first + jnp.arange(depth_planes, dtype=jnp.int32)
    at_receivers = (global_plane == 2).astype(jnp.float32)[:, None, None]
    current = adj_now[0]
    older = adj_prev[0]
    for step in range(steps):
        moment = steps - 1 - step
        rimmed_field = with_halo(current[None], (("depth", 1),), 1)[0]
        plane = source_plane(rows_x, rows_y, residual[0, moment], width_x, width_y)
        spread = operate(rimmed_field, buoy_ext)[1:-1]
        newer = (
            2.0 * current - older + 0.08 * kappa_ext * spread + 0.08 * at_receivers * plane[None]
        )
        image = image + snaps[moment].astype(jnp.float32) * newer
        older = current
        current = newer
    weighted = shot_count[0].astype(jnp.float32) * image
    summed = lax.psum_scatter(weighted, "shots", scatter_dimension=1, tiled=True)
    grad_vel = 2.0 * density * velocity * summed / (4.0 * groups)
    return (current[None], older[None], grad_vel)


def solution(mesh):
    in_specs = (
        P("shots", "depth", None, None),
        P("shots", "depth", None, None),
        P("shots", None, "depth", None, None),
        P("depth", "shots", None),
        P("depth", "shots", None),
        P("shots"),
        P("shots", None),
        P("shots", None),
        P("shots", None, None),
    )
    out_specs = (
        P("shots", "depth", None, None),
        P("shots", "depth", None, None),
        P("depth", "shots", None),
    )
    return jax.shard_map(body, mesh=mesh, in_specs=in_specs, out_specs=out_specs, check_vma=False)
```

profile of v0, /device:TPU:2, one launch (start us, length us, event | category | flops | bytes accessed | tf_op | source)
XLA Modules:
  0.0 387.4 jit_solution(11470372513918090008)
XLA Ops:
  7.2 0.0 all-gather.5.cloned.1.call-start
  7.2 1.4 copy.15
  8.6 0.0 all-gather.5.cloned.1.call-update
  8.6 0.0 all-gather.3.cloned.1.call-start
  8.7 1.4 copy.14
  10.1 0.0 all-gather.3.cloned.1.call-update
  10.1 0.0 reduce-scatter.2.cloned.1.call-start
  10.1 0.9 fusion.106
  11.0 4.2 %collective-permute-start.3 = (f32[1,1,128,128]{3,1,2,0:T(1,128)S(1)}, f32[1,1,128,128]{3,1,2,0:T(1,128)S(1)}, u32[]{:S(2)}, u32[]{:S(2)}) collective-permute-start(f32[1,1,128,128]{3,1,2,0:T(1,128)S(1)} %bitcast.68), channel_id=1, source_target_pairs={{32,0},{64,32},{96,64},{128,96},{160,128},{192,160},{224,192},{33,... | collective-permute-start | bytes 196616 | tf_op jit(solution)/shard_map/ppermute | solution.py:15
  15.2 1.9 collective-permute-start.2
  17.1 1.8 copy.12
  19.0 0.4 fusion.79
  19.4 2.9 fusion.102
  22.3 0.2 maximum_bitcast_fusion
  22.6 54.4 %all-gather.5.cloned.1.call-done = f32[16,128,128]{2,0,1:T(8,128)} async-done(((f32[16,4,128]{2,0,1:T(8,128)}), f32[16,128,128]{2,0,1:T(8,128)}) %all-gather.5.cloned.1.call-update) | async-done | bytes 1048592 | tf_op jit(solution)/shard_map/all_gather | solution.py:54
  77.0 65.7 %all-gather.3.cloned.1.call-done = f32[16,128,128]{2,0,1:T(8,128)} async-done(((f32[16,4,128]{2,0,1:T(8,128)}), f32[16,128,128]{2,0,1:T(8,128)}) %all-gather.3.cloned.1.call-update) | async-done | bytes 1048592 | tf_op jit(solution)/shard_map/all_gather | solution.py:55
  142.7 1.7 multiply_multiply_fusion
  144.4 0.2 pad_maximum_fusion.4
  144.6 2.5 collective-permute-start.1
  147.1 3.4 collective-permute-start
  150.5 4.5 %fusion.12 = (f32[18,128,128]{2,0,1:T(8,128)}, f32[18,128,128]{2,0,1:T(8,128)}, f32[18,128,128]{2,0,1:T(8,128)}, f32[18,128,128]{2,0,1:T(8,128)}, f32[18,128,128]{2,0,1:T(8,128)}, /*index=5*/f32[18,128,128]{2,0,1:T(8,128)}) fusion(f32[18,128,128]{2,0,1:T(8,128)S(1)} %maximum_bitcast_fusion), kind=kLoop, calls=%fused_computation.42 | loop fusion | flops 589824 | bytes 8257536 | tf_op jit(solution)/shard_map/sub | solution.py:32
  155.0 0.0 copy-start.13
  155.0 0.2 fusion.20
  155.3 0.0 copy-start.5
  155.3 1.3 fusion.1
  156.6 0.0 copy-done.13
  156.7 0.6 copy-done.4
  157.3 0.3 copy-done.5
  157.6 1.5 copy-done.6
  159.0 0.6 copy-done.7
  159.6 0.4 copy-done.8
  160.1 0.4 copy-done.9
  160.5 0.4 copy-done.10
  161.0 4.0 %fusion.61 = f32[16,128,128]{2,0,1:T(8,128)S(1)} fusion(f32[18,128,128]{2,0,1:T(8,128)S(1)} %copy-done.9, f32[18,128,128]{2,0,1:T(8,128)S(1)} %copy-done.8, f32[18,128,128]{2,0,1:T(8,128)S(1)} %copy-done.7, f32[18,128,128]{2,0,1:T(8,128)S(1)} %copy-done.11, f32[18,128,128]{2,0,1:T(8,128)S(1)} %copy-done.4, f32[18,128,128]{2,0,1:T(8,128)S(1)} %copy-done.10, ...), kind=kLoop, calls=%fused_computation.118 | loop fusion | flops 5767168 | bytes 17891392 | tf_op jit(solution)/shard_map/add | solution.py:76
  165.0 0.1 fusion.105
  165.1 2.5 collective-permute-start.5
  167.6 3.4 collective-permute-start.4
  170.9 0.4 fusion.77
  171.4 2.4 collective-permute-done.4
  173.7 1.4 maximum_bitcast_fusion.1
  175.1 10.0 %fusion.14 = (f32[18,128,128]{2,0,1:T(8,128)}, f32[18,128,128]{2,0,1:T(8,128)}, f32[18,128,128]{2,0,1:T(8,128)}, f32[18,128,128]{2,0,1:T(8,128)}, f32[18,128,128]{2,0,1:T(8,128)}, /*index=5*/f32[18,128,128]{2,0,1:T(8,128)}) fusion(f32[18,128,128]{2,0,1:T(8,128)} %maximum_bitcast_fusion.1), kind=kLoop, calls=%fused_computation.44 | loop fusion | flops 589824 | bytes 8257536 | tf_op jit(solution)/shard_map/sub | solution.py:32
  185.1 6.6 %fusion.49 = f32[16,128,128]{2,0,1:T(8,128)S(1)} fusion(f32[18,128,128]{2,0,1:T(8,128)} %get-tuple-element.29, f32[18,128,128]{2,0,1:T(8,128)} %get-tuple-element.28, f32[18,128,128]{2,0,1:T(8,128)} %get-tuple-element.27, f32[18,128,128]{2,0,1:T(8,128)} %get-tuple-element.31, f32[18,128,128]{2,0,1:T(8,128)} %maximum_bitcast_fusion.1, ...), kind=kLoop, calls=%fused_computation.100 | loop fusion | flops 5767168 | bytes 17891392 | tf_op jit(solution)/shard_map/add | solution.py:76
  191.7 0.1 fusion.104
  191.8 1.9 collective-permute-start.7
  193.7 5.4 %collective-permute-start.6 = (f32[1,1,128,128]{3,1,2,0:T(1,128)S(1)}, f32[1,1,128,128]{3,1,2,0:T(1,128)S(1)}, u32[]{:S(2)}, u32[]{:S(2)}) collective-permute-start(f32[1,1,128,128]{3,1,2,0:T(1,128)S(1)} %get-tuple-element.46), channel_id=1, source_target_pairs={{0,32},{32,64},{64,96},{96,128},{128,160},{160,192},{192,224},{1,3... | collective-permute-start | bytes 196616 | tf_op jit(solution)/shard_map/ppermute | solution.py:14
  199.2 0.4 fusion.75
  199.6 1.3 collective-permute-done.6
  200.9 1.4 maximum_bitcast_fusion.2
  202.3 10.0 %fusion.16 = (f32[18,128,128]{2,0,1:T(8,128)}, f32[18,128,128]{2,0,1:T(8,128)}, f32[18,128,128]{2,0,1:T(8,128)}, f32[18,128,128]{2,0,1:T(8,128)}, f32[18,128,128]{2,0,1:T(8,128)}, /*index=5*/f32[18,128,128]{2,0,1:T(8,128)}) fusion(f32[18,128,128]{2,0,1:T(8,128)} %maximum_bitcast_fusion.2), kind=kLoop, calls=%fused_computation.46 | loop fusion | flops 589824 | bytes 8257536 | tf_op jit(solution)/shard_map/sub | solution.py:32
  212.3 6.5 %fusion.37 = f32[16,128,128]{2,0,1:T(8,128)S(1)} fusion(f32[18,128,128]{2,0,1:T(8,128)} %get-tuple-element.23, f32[18,128,128]{2,0,1:T(8,128)} %get-tuple-element.22, f32[18,128,128]{2,0,1:T(8,128)} %get-tuple-element.21, f32[18,128,128]{2,0,1:T(8,128)} %get-tuple-element.25, f32[18,128,128]{2,0,1:T(8,128)} %maximum_bitcast_fusion.2, ...), kind=kLoop, calls=%fused_computation.82 | loop fusion | flops 5767168 | bytes 17891392 | tf_op jit(solution)/shard_map/add | solution.py:76
  218.8 0.1 fusion.103
  218.9 1.9 collective-permute-start.9
  220.9 7.5 %collective-permute-start.8 = (f32[1,1,128,128]{3,1,2,0:T(1,128)S(1)}, f32[1,1,128,128]{3,1,2,0:T(1,128)S(1)}, u32[]{:S(2)}, u32[]{:S(2)}) collective-permute-start(f32[1,1,128,128]{3,1,2,0:T(1,128)S(1)} %get-tuple-element.44), channel_id=1, source_target_pairs={{0,32},{32,64},{64,96},{96,128},{128,160},{160,192},{192,224},{1,3... | collective-permute-start | bytes 196616 | tf_op jit(solution)/shard_map/ppermute | solution.py:14
  228.4 0.4 fusion.73
  229.5 0.8 collective-permute-done.8
  230.3 1.4 maximum_bitcast_fusion.3
  231.7 10.0 %fusion.18 = (f32[18,128,128]{2,0,1:T(8,128)}, f32[18,128,128]{2,0,1:T(8,128)}, f32[18,128,128]{2,0,1:T(8,128)}, f32[18,128,128]{2,0,1:T(8,128)}, f32[18,128,128]{2,0,1:T(8,128)}, /*index=5*/f32[18,128,128]{2,0,1:T(8,128)}) fusion(f32[18,128,128]{2,0,1:T(8,128)} %maximum_bitcast_fusion.3), kind=kLoop, calls=%fused_computation.48 | loop fusion | flops 589824 | bytes 8257536 | tf_op jit(solution)/shard_map/sub | solution.py:32
  241.7 9.0 %fusion.70 = (f32[16,128,128]{2,0,1:T(8,128)}, f32[16,128,128]{2,0,1:T(8,128)}) fusion(f32[16,128,128]{2,0,1:T(8,128)S(1)} %fusion.37, f32[16,128,128]{2,0,1:T(8,128)} %copy-done.2, f32[16,128,128]{2,0,1:T(8,128)S(1)} %fusion.61, bf16[1,1,16,128,128]{4,3,2,1,0:T(8,128)(2,1)} %get-tuple-element.11, bf16[1,1,16,128,128]{4,3,2,1,0:T(8,128)(2,1)} %get-tuple-element.9, ...), kind=kLoop, calls=%fused_computation.133 | loop fusion | flops 8912896 | bytes 22085700 | tf_op jit(solution)/shard_map/mul | solution.py:81
  250.7 0.0 reduce-scatter.2.cloned.1.call-update
  250.7 1.3 copy.26
  252.0 1.3 copy.25
  253.3 126.2 %reduce-scatter.2.cloned.1.call-done = f32[16,4,128]{2,0,1:T(8,128)} async-done(((f32[16,128,128]{2,0,1:T(8,128)}), f32[16,4,128]{2,0,1:T(8,128)}) %reduce-scatter.2.cloned.1.call-update) | async-done | bytes 32784 | tf_op jit(solution)/shard_map/reduce_scatter | solution.py:82
  379.5 0.8 multiply_multiply_fusion.1
  380.3 0.6 copy.27
  (37 shorter events, 0.1 us)
Async XLA Ops:
  7.2 11.8 %copy-start.16 = (f32[1,4,256]{2,1,0:T(4,128)S(1)}, f32[1,4,256]{2,1,0:T(4,128)}, u32[]{:S(2)}) copy-start(f32[1,4,256]{2,1,0:T(4,128)} %param.17) | copy-start | bytes 12292
  7.2 11.8 %copy-start.17 = (s32[1,256]{1,0:T(1,128)S(1)}, s32[1,256]{1,0:T(1,128)}, u32[]{:S(2)}) copy-start(s32[1,256]{1,0:T(1,128)} %param.16) | copy-start | bytes 3076
  7.2 11.8 %copy-start.18 = (s32[1,256]{1,0:T(1,128)S(1)}, s32[1,256]{1,0:T(1,128)}, u32[]{:S(2)}) copy-start(s32[1,256]{1,0:T(1,128)} %param.15) | copy-start | bytes 3076
  7.2 69.8 %all-gather.5.cloned.1.call-start = ((), (), s32[]{:S(2)}) async-start(), calls=%async_computation.2 | async-start | bytes 1081344 | tf_op jit(solution)/shard_map/all_gather | solution.py:54
  8.6 134.0 %all-gather.3.cloned.1.call-start = ((), (), s32[]{:S(2)}) async-start(), calls=%async_computation.1 | async-start | bytes 1081344 | tf_op jit(solution)/shard_map/all_gather | solution.py:55
  10.1 369.4 %reduce-scatter.2.cloned.1.call-start = ((), (), s32[]{:S(2)}) async-start(), calls=%async_computation.3 | async-start | bytes 1081344 | tf_op jit(solution)/shard_map/reduce_scatter | solution.py:82
  11.0 11.3 %collective-permute-start.3 = (f32[1,1,128,128]{3,1,2,0:T(1,128)S(1)}, f32[1,1,128,128]{3,1,2,0:T(1,128)S(1)}, u32[]{:S(2)}, u32[]{:S(2)}) collective-permute-start(f32[1,1,128,128]{3,1,2,0:T(1,128)S(1)} %bitcast.68), channel_id=1, source_target_pairs={{32,0},{64,32},{96,64},{128,96},{160,128},{192,160},{224,192},{33,... | collective-permute-start | bytes 196616 | tf_op jit(solution)/shard_map/ppermute | solution.py:15
  15.2 7.1 %collective-permute-start.2 = (f32[1,1,128,128]{3,1,2,0:T(1,128)S(1)}, f32[1,1,128,128]{3,1,2,0:T(1,128)S(1)}, u32[]{:S(2)}, u32[]{:S(2)}) collective-permute-start(f32[1,1,128,128]{3,1,2,0:T(1,128)S(1)} %bitcast.67), channel_id=1, source_target_pairs={{0,32},{32,64},{64,96},{96,128},{128,160},{160,192},{192,224},{1,3... | collective-permute-start | bytes 196616 | tf_op jit(solution)/shard_map/ppermute | solution.py:14
  22.6 127.9 %copy-start.3 = (f32[18,128,128]{2,0,1:T(8,128)}, f32[18,128,128]{2,0,1:T(8,128)S(1)}, u32[]{:S(2)}) copy-start(f32[18,128,128]{2,0,1:T(8,128)S(1)} %maximum_bitcast_fusion) | copy-start | bytes 3538948
  144.6 10.4 %collective-permute-start.1 = (f32[2,1,128,128]{3,1,2,0:T(1,128)S(1)}, f32[2,1,128,128]{3,1,2,0:T(1,128)S(1)}, u32[]{:S(2)}, u32[]{:S(2)}) collective-permute-start(f32[2,1,128,128]{3,1,2,0:T(1,128)S(1)} %get-tuple-element.13), channel_id=1, source_target_pairs={{32,0},{64,32},{96,64},{128,96},{160,128},{192,160},{224,192},{33,... | collective-permute-start | bytes 393224 | tf_op jit(solution)/shard_map/ppermute | solution.py:15
  147.1 7.9 %collective-permute-start = (f32[2,1,128,128]{3,1,2,0:T(1,128)S(1)}, f32[2,1,128,128]{3,1,2,0:T(1,128)S(1)}, u32[]{:S(2)}, u32[]{:S(2)}) collective-permute-start(f32[2,1,128,128]{3,1,2,0:T(1,128)S(1)} %get-tuple-element.12), channel_id=1, source_target_pairs={{0,32},{32,64},{64,96},{96,128},{128,160},{160,192},{192,224},{1,3... | collective-permute-start | bytes 393224 | tf_op jit(solution)/shard_map/ppermute | solution.py:14
  155.0 1.6 copy-start.11
  155.0 1.7 copy-start.13
  155.3 2.0 copy-start.4
  155.3 2.3 copy-start.5
  155.3 3.7 copy-start.6
  155.3 4.3 %copy-start.7 = (f32[18,128,128]{2,0,1:T(8,128)S(1)}, f32[18,128,128]{2,0,1:T(8,128)}, u32[]{:S(2)}) copy-start(f32[18,128,128]{2,0,1:T(8,128)} %get-tuple-element.39) | copy-start | bytes 3538948
  155.3 4.8 %copy-start.8 = (f32[18,128,128]{2,0,1:T(8,128)S(1)}, f32[18,128,128]{2,0,1:T(8,128)}, u32[]{:S(2)}) copy-start(f32[18,128,128]{2,0,1:T(8,128)} %get-tuple-element.40) | copy-start | bytes 3538948
  155.3 5.2 %copy-start.9 = (f32[18,128,128]{2,0,1:T(8,128)S(1)}, f32[18,128,128]{2,0,1:T(8,128)}, u32[]{:S(2)}) copy-start(f32[18,128,128]{2,0,1:T(8,128)} %get-tuple-element.41) | copy-start | bytes 3538948
  155.3 5.7 %copy-start.10 = (f32[18,128,128]{2,0,1:T(8,128)S(1)}, f32[18,128,128]{2,0,1:T(8,128)}, u32[]{:S(2)}) copy-start(f32[18,128,128]{2,0,1:T(8,128)} %get-tuple-element.42) | copy-start | bytes 3538948
  156.6 8.3 %copy-start = (f32[18,128,128]{2,0,1:T(8,128)}, f32[18,128,128]{2,0,1:T(8,128)S(1)}, u32[]{:S(2)}) copy-start(f32[18,128,128]{2,0,1:T(8,128)S(1)} %get-tuple-element.36) | copy-start | bytes 3538948
  156.6 8.3 %copy-start.1 = (f32[18,128,128]{2,0,1:T(8,128)}, f32[18,128,128]{2,0,1:T(8,128)S(1)}, u32[]{:S(2)}) copy-start(f32[18,128,128]{2,0,1:T(8,128)S(1)} %get-tuple-element.37) | copy-start | bytes 3538948
  165.1 6.3 %collective-permute-start.5 = (f32[1,1,128,128]{3,1,2,0:T(1,128)S(1)}, f32[1,1,128,128]{3,1,2,0:T(1,128)S(1)}, u32[]{:S(2)}, u32[]{:S(2)}) collective-permute-start(f32[1,1,128,128]{3,1,2,0:T(1,128)S(1)} %get-tuple-element.49), channel_id=1, source_target_pairs={{32,0},{64,32},{96,64},{128,96},{160,128},{192,160},{224,192},{33,... | collective-permute-start | bytes 196616 | tf_op jit(solution)/shard_map/ppermute | solution.py:15
  167.6 6.2 %collective-permute-start.4 = (f32[1,1,128,128]{3,1,2,0:T(1,128)S(1)}, f32[1,1,128,128]{3,1,2,0:T(1,128)S(1)}, u32[]{:S(2)}, u32[]{:S(2)}) collective-permute-start(f32[1,1,128,128]{3,1,2,0:T(1,128)S(1)} %get-tuple-element.48), channel_id=1, source_target_pairs={{0,32},{32,64},{64,96},{96,128},{128,160},{160,192},{192,224},{1,3... | collective-permute-start | bytes 196616 | tf_op jit(solution)/shard_map/ppermute | solution.py:14
  191.7 9.2 %copy-start.2 = (f32[16,128,128]{2,0,1:T(8,128)}, f32[16,128,128]{2,0,1:T(8,128)S(1)}, u32[]{:S(2)}) copy-start(f32[16,128,128]{2,0,1:T(8,128)S(1)} %fusion.49) | copy-start | bytes 3145732
  191.8 7.8 %collective-permute-start.7 = (f32[1,1,128,128]{3,1,2,0:T(1,128)S(1)}, f32[1,1,128,128]{3,1,2,0:T(1,128)S(1)}, u32[]{:S(2)}, u32[]{:S(2)}) collective-permute-start(f32[1,1,128,128]{3,1,2,0:T(1,128)S(1)} %get-tuple-element.47), channel_id=1, source_target_pairs={{32,0},{64,32},{96,64},{128,96},{160,128},{192,160},{224,192},{33,... | collective-permute-start | bytes 196616 | tf_op jit(solution)/shard_map/ppermute | solution.py:15
  193.7 7.1 %collective-permute-start.6 = (f32[1,1,128,128]{3,1,2,0:T(1,128)S(1)}, f32[1,1,128,128]{3,1,2,0:T(1,128)S(1)}, u32[]{:S(2)}, u32[]{:S(2)}) collective-permute-start(f32[1,1,128,128]{3,1,2,0:T(1,128)S(1)} %get-tuple-element.46), channel_id=1, source_target_pairs={{0,32},{32,64},{64,96},{96,128},{128,160},{160,192},{192,224},{1,3... | collective-permute-start | bytes 196616 | tf_op jit(solution)/shard_map/ppermute | solution.py:14
  218.9 10.5 %collective-permute-start.9 = (f32[1,1,128,128]{3,1,2,0:T(1,128)S(1)}, f32[1,1,128,128]{3,1,2,0:T(1,128)S(1)}, u32[]{:S(2)}, u32[]{:S(2)}) collective-permute-start(f32[1,1,128,128]{3,1,2,0:T(1,128)S(1)} %get-tuple-element.45), channel_id=1, source_target_pairs={{32,0},{64,32},{96,64},{128,96},{160,128},{192,160},{224,192},{33,... | collective-permute-start | bytes 196616 | tf_op jit(solution)/shard_map/ppermute | solution.py:15
  220.9 9.4 %collective-permute-start.8 = (f32[1,1,128,128]{3,1,2,0:T(1,128)S(1)}, f32[1,1,128,128]{3,1,2,0:T(1,128)S(1)}, u32[]{:S(2)}, u32[]{:S(2)}) collective-permute-start(f32[1,1,128,128]{3,1,2,0:T(1,128)S(1)} %get-tuple-element.44), channel_id=1, source_target_pairs={{0,32},{32,64},{64,96},{96,128},{128,160},{160,192},{192,224},{1,3... | collective-permute-start | bytes 196616 | tf_op jit(solution)/shard_map/ppermute | solution.py:14
  250.6 1.3 copy-start.12
  252.0 127.5 %copy-start.14 = (f32[16,4,128]{2,1,0:T(4,128)S(1)}, f32[16,4,128]{2,1,0:T(4,128)}, u32[]{:S(2)}) copy-start(f32[16,4,128]{2,1,0:T(4,128)} %param.12) | copy-start | bytes 98308
  252.0 127.5 %copy-start.15 = (f32[16,4,128]{2,1,0:T(4,128)S(1)}, f32[16,4,128]{2,1,0:T(4,128)}, u32[]{:S(2)}) copy-start(f32[16,4,128]{2,1,0:T(4,128)} %param.13) | copy-start | bytes 98308
Sparse Core Ops, SparseCore 0:
  10.4 66.4 all-gather.4
  79.4 63.2 all-gather.2
  250.8 128.6 reduce-scatter.1
where the time goes:
time: 388 us; the launch traced here: 387 us
  waiting for transfers between devices  251 us (65%)
  other arithmetic  69.2 us (18%)
  starting transfers between devices  34.7 us (9%)
  local copies, waits for them, and re-layouts  16.3 us (4%)
  between operations  14.9 us (4%)
    reduce_scatter x1, waiting for transfers between devices, body(): lax.psum_scatter(weighted, 'shots', scatter_dimension=1, tiled=True)  126 us
    all_gather x1, waiting for transfers between devices, body(): lax.all_gather(density, 'shots', axis=1, tiled=True)  65.7 us
    all_gather x1, waiting for transfers between devices, body(): lax.all_gather(velocity, 'shots', axis=1, tiled=True)  54.4 us
    sub x4, other arithmetic, operate(): total = total + 0.5 * (bc + ba) * (pa - pc) - 0.5 * (bb + bc) * (pc - pb)  34.5 us
    ppermute x5, starting transfers between devices, with_halo(): before = lax.ppermute(last, axis, up)  21.6 us
    add x3, other arithmetic, body(): 2.0 * current - older + 0.08 * kappa_ext * spread  17.1 us
    ppermute x5, starting transfers between devices, with_halo(): after = lax.ppermute(first, axis, down)  12.9 us
    unnamed x44, local copies, waits for them, and re-layouts  12.2 us
  transfers between devices with their start and end apart: 13, of which 6 were waited for; matrix products, arithmetic and copies ran while one was open for 4% of the time, Pallas kernels for 0%

commit v1 on v0

--- a/solution.py
+++ b/solution.py
@@ -50,8 +50,18 @@
     steps = fwd_snap.shape[1]
     groups = lax.axis_size("shots")
     width = 1
+
+    def rounds_update(page):
+        v1 = jnp.concatenate(
+            lax.all_to_all(
+                jnp.stack(tuple((page for _ in range(lax.axis_size("shots"))))), "shots", 0, 0
+            ),
+            axis=1,
+        )
+        return v1
+
     vel_all, rho_all = (
-        lax.all_gather(velocity, "shots", axis=1, tiled=True),
+        rounds_update(velocity),
         lax.all_gather(density, "shots", axis=1, tiled=True),
     )
     packed = jnp.stack([rho_all * vel_all * vel_all, 1.0 / rho_all])

time: 388 us -> 333 us (0.86)
  waiting for transfers between devices: 251 us -> 186 us
  starting transfers between devices: 34.7 us -> 44.5 us
    all_gather x1 -> x0, waiting for transfers between devices: 54.4 us -> none  [body(): lax.all_gather(velocity, 'shots', axis=1, tiled=True)]
    all_gather x1, waiting for transfers between devices: 65.7 us -> 37 us  [body(): lax.all_gather(density, 'shots', axis=1, tiled=True)]
    all_to_all x0 -> x1, waiting for transfers between devices: none -> 18.5 us  [rounds_update(): lax.all_to_all(jnp.stack(tuple((page for _ in range(lax.axis_size('shots'...]
    all_to_all x0 -> x1, starting transfers between devices: none -> 10 us  [rounds_update(): lax.all_to_all(jnp.stack(tuple((page for _ in range(lax.axis_size('shots'...]
    unnamed x44 -> x49, local copies, waits for them, and re-layouts: 12.2 us -> 10.3 us
where the time goes in v1:
time: 333 us
  waiting for transfers between devices  186 us (56%)
  other arithmetic  69.3 us (21%)
  starting transfers between devices  44.5 us (13%)
  local copies, waits for them, and re-layouts  16.3 us (5%)
  between operations  15.2 us (5%)
    reduce_scatter x1, waiting for transfers between devices, body(): lax.psum_scatter(weighted, 'shots', scatter_dimension=1, tiled=True)  126 us
    all_gather x1, waiting for transfers between devices, body(): lax.all_gather(density, 'shots', axis=1, tiled=True)  37 us
    sub x4, other arithmetic, operate(): total = total + 0.5 * (bc + ba) * (pa - pc) - 0.5 * (bb + bc) * (pc - pb)  34.7 us
    ppermute x5, starting transfers between devices, with_halo(): before = lax.ppermute(last, axis, up)  23.3 us
    all_to_all x1, waiting for transfers between devices, rounds_update(): lax.all_to_all(jnp.stack(tuple((page for _ in range(lax.axis_size('shots'...  18.5 us
    add x3, other arithmetic, body(): 2.0 * current - older + 0.08 * kappa_ext * spread  17 us
    ppermute x5, starting transfers between devices, with_halo(): after = lax.ppermute(first, axis, down)  11.1 us
    unnamed x49, local copies, waits for them, and re-layouts  10.3 us
  transfers between devices with their start and end apart: 13, of which 6 were waited for; matrix products, arithmetic and copies ran while one was open for 4% of the time, Pallas kernels for 0%

profile of v1, /device:TPU:2, one launch (start us, length us, event | category | flops | bytes accessed | tf_op | source)
XLA Modules:
  0.0 332.6 jit_solution(8144369450489569510)
XLA Ops:
  7.2 0.0 copy-start.5
  7.2 2.1 stack.8
  9.2 10.0 %all-to-all-start = ((f32[32,16,4,128]{3,2,1,0:T(4,128)}), f32[32,16,4,128]{3,2,1,0:T(4,128)}, u32[]{:S(2)}, u32[]{:S(2)}) async-start(f32[32,16,4,128]{3,2,1,0:T(4,128)} %stack.8), calls=%async_computation | async-start | bytes 2097152 | tf_op jit(solution)/shard_map/all_to_all | solution.py:56
  19.2 0.0 copy-start.19
  19.3 0.0 all-gather.2.cloned.1.call-start
  19.4 0.6 copy.14
  20.0 0.1 all-gather.2.cloned.1.call-update
  20.0 0.0 reduce-scatter.2.cloned.1.call-start
  20.1 2.4 collective-permute-start.3
  22.6 3.4 %collective-permute-start.2 = (f32[1,1,128,128]{3,1,2,0:T(1,128)S(1)}, f32[1,1,128,128]{3,1,2,0:T(1,128)S(1)}, u32[]{:S(2)}, u32[]{:S(2)}) collective-permute-start(f32[1,1,128,128]{3,1,2,0:T(1,128)S(1)} %bitcast.70), channel_id=1, source_target_pairs={{0,32},{32,64},{64,96},{96,128},{128,160},{160,192},{192,224},{1,3... | collective-permute-start | bytes 196616 | tf_op jit(solution)/shard_map/ppermute | solution.py:14
  26.0 1.6 copy.12
  27.6 0.4 fusion.79
  28.0 1.3 fusion.104
  29.4 0.5 copy-done.14
  29.8 0.2 maximum_bitcast_fusion
  30.1 18.5 %all-to-all-done = f32[32,16,4,128]{3,2,1,0:T(4,128)} async-done(((f32[32,16,4,128]{3,2,1,0:T(4,128)}), f32[32,16,4,128]{3,2,1,0:T(4,128)}, u32[]{:S(2)}, u32[]{:S(2)}) %all-to-all-start) | async-done | bytes 1048608 | tf_op jit(solution)/shard_map/all_to_all | solution.py:56
  48.5 2.3 copy.15
  50.8 37.0 %all-gather.2.cloned.1.call-done = f32[16,128,128]{2,0,1:T(8,128)} async-done(((f32[16,4,128]{2,0,1:T(8,128)}), f32[16,128,128]{2,0,1:T(8,128)}) %all-gather.2.cloned.1.call-update) | async-done | bytes 1048592 | tf_op jit(solution)/shard_map/all_gather | solution.py:65
  87.9 1.7 multiply_multiply_fusion
  89.6 0.2 pad_maximum_fusion.4
  89.8 2.4 collective-permute-start.1
  92.2 3.4 %collective-permute-start = (f32[2,1,128,128]{3,1,2,0:T(1,128)S(1)}, f32[2,1,128,128]{3,1,2,0:T(1,128)S(1)}, u32[]{:S(2)}, u32[]{:S(2)}) collective-permute-start(f32[2,1,128,128]{3,1,2,0:T(1,128)S(1)} %get-tuple-element.12), channel_id=1, source_target_pairs={{0,32},{32,64},{64,96},{96,128},{128,160},{160,192},{192,224},{1,3... | collective-permute-start | bytes 393224 | tf_op jit(solution)/shard_map/ppermute | solution.py:14
  95.7 4.5 %fusion.12 = (f32[18,128,128]{2,0,1:T(8,128)}, f32[18,128,128]{2,0,1:T(8,128)}, f32[18,128,128]{2,0,1:T(8,128)}, f32[18,128,128]{2,0,1:T(8,128)}, f32[18,128,128]{2,0,1:T(8,128)}, /*index=5*/f32[18,128,128]{2,0,1:T(8,128)}) fusion(f32[18,128,128]{2,0,1:T(8,128)S(1)} %maximum_bitcast_fusion), kind=kLoop, calls=%fused_computation.42 | loop fusion | flops 589824 | bytes 8257536 | tf_op jit(solution)/shard_map/sub | solution.py:32
  100.2 0.2 fusion.20
  100.6 1.3 fusion.1
  101.9 0.0 copy-done.16
  101.9 0.6 copy-done.4
  102.5 0.3 copy-done.6
  102.8 1.5 copy-done.7
  104.2 0.6 copy-done.8
  104.9 0.4 copy-done.9
  105.3 0.4 copy-done.10
  105.8 0.4 copy-done.11
  106.2 3.9 %fusion.61 = f32[16,128,128]{2,0,1:T(8,128)S(1)} fusion(f32[18,128,128]{2,0,1:T(8,128)S(1)} %copy-done.10, f32[18,128,128]{2,0,1:T(8,128)S(1)} %copy-done.9, f32[18,128,128]{2,0,1:T(8,128)S(1)} %copy-done.8, f32[18,128,128]{2,0,1:T(8,128)S(1)} %copy-done.12, f32[18,128,128]{2,0,1:T(8,128)S(1)} %copy-done.4, f32[18,128,128]{2,0,1:T(8,128)S(1)} %copy-done.11, ...), kind=kLoop, calls=%fused_computation.118 | loop fusion | flops 5767168 | bytes 17891392 | tf_op jit(solution)/shard_map/add | solution.py:86
  110.2 0.1 fusion.107
  110.3 2.4 collective-permute-start.5
  112.7 3.4 %collective-permute-start.4 = (f32[1,1,128,128]{3,1,2,0:T(1,128)S(1)}, f32[1,1,128,128]{3,1,2,0:T(1,128)S(1)}, u32[]{:S(2)}, u32[]{:S(2)}) collective-permute-start(f32[1,1,128,128]{3,1,2,0:T(1,128)S(1)} %get-tuple-element.48), channel_id=1, source_target_pairs={{0,32},{32,64},{64,96},{96,128},{128,160},{160,192},{192,224},{1,3... | collective-permute-start | bytes 196616 | tf_op jit(solution)/shard_map/ppermute | solution.py:14
  116.1 0.4 fusion.77
  116.6 2.3 collective-permute-done.4
  118.9 1.4 maximum_bitcast_fusion.1
  120.3 10.1 %fusion.14 = (f32[18,128,128]{2,0,1:T(8,128)}, f32[18,128,128]{2,0,1:T(8,128)}, f32[18,128,128]{2,0,1:T(8,128)}, f32[18,128,128]{2,0,1:T(8,128)}, f32[18,128,128]{2,0,1:T(8,128)}, /*index=5*/f32[18,128,128]{2,0,1:T(8,128)}) fusion(f32[18,128,128]{2,0,1:T(8,128)} %maximum_bitcast_fusion.1), kind=kLoop, calls=%fused_computation.44 | loop fusion | flops 589824 | bytes 8257536 | tf_op jit(solution)/shard_map/sub | solution.py:32
  130.3 6.5 %fusion.49 = f32[16,128,128]{2,0,1:T(8,128)S(1)} fusion(f32[18,128,128]{2,0,1:T(8,128)} %get-tuple-element.29, f32[18,128,128]{2,0,1:T(8,128)} %get-tuple-element.28, f32[18,128,128]{2,0,1:T(8,128)} %get-tuple-element.27, f32[18,128,128]{2,0,1:T(8,128)} %get-tuple-element.31, f32[18,128,128]{2,0,1:T(8,128)} %maximum_bitcast_fusion.1, ...), kind=kLoop, calls=%fused_computation.100 | loop fusion | flops 5767168 | bytes 17891392 | tf_op jit(solution)/shard_map/add | solution.py:86
  136.9 0.1 fusion.106
  137.0 1.9 collective-permute-start.7
  138.9 5.5 %collective-permute-start.6 = (f32[1,1,128,128]{3,1,2,0:T(1,128)S(1)}, f32[1,1,128,128]{3,1,2,0:T(1,128)S(1)}, u32[]{:S(2)}, u32[]{:S(2)}) collective-permute-start(f32[1,1,128,128]{3,1,2,0:T(1,128)S(1)} %get-tuple-element.46), channel_id=1, source_target_pairs={{0,32},{32,64},{64,96},{96,128},{128,160},{160,192},{192,224},{1,3... | collective-permute-start | bytes 196616 | tf_op jit(solution)/shard_map/ppermute | solution.py:14
  144.5 0.4 fusion.75
  144.9 1.3 collective-permute-done.6
  146.2 1.4 maximum_bitcast_fusion.2
  147.6 10.1 %fusion.16 = (f32[18,128,128]{2,0,1:T(8,128)}, f32[18,128,128]{2,0,1:T(8,128)}, f32[18,128,128]{2,0,1:T(8,128)}, f32[18,128,128]{2,0,1:T(8,128)}, f32[18,128,128]{2,0,1:T(8,128)}, /*index=5*/f32[18,128,128]{2,0,1:T(8,128)}) fusion(f32[18,128,128]{2,0,1:T(8,128)} %maximum_bitcast_fusion.2), kind=kLoop, calls=%fused_computation.46 | loop fusion | flops 589824 | bytes 8257536 | tf_op jit(solution)/shard_map/sub | solution.py:32
  157.6 6.5 %fusion.37 = f32[16,128,128]{2,0,1:T(8,128)S(1)} fusion(f32[18,128,128]{2,0,1:T(8,128)} %get-tuple-element.23, f32[18,128,128]{2,0,1:T(8,128)} %get-tuple-element.22, f32[18,128,128]{2,0,1:T(8,128)} %get-tuple-element.21, f32[18,128,128]{2,0,1:T(8,128)} %get-tuple-element.25, f32[18,128,128]{2,0,1:T(8,128)} %maximum_bitcast_fusion.2, ...), kind=kLoop, calls=%fused_computation.82 | loop fusion | flops 5767168 | bytes 17891392 | tf_op jit(solution)/shard_map/add | solution.py:86
  164.1 0.1 fusion.105
  164.2 1.9 collective-permute-start.9
  166.2 7.5 %collective-permute-start.8 = (f32[1,1,128,128]{3,1,2,0:T(1,128)S(1)}, f32[1,1,128,128]{3,1,2,0:T(1,128)S(1)}, u32[]{:S(2)}, u32[]{:S(2)}) collective-permute-start(f32[1,1,128,128]{3,1,2,0:T(1,128)S(1)} %get-tuple-element.44), channel_id=1, source_target_pairs={{0,32},{32,64},{64,96},{96,128},{128,160},{160,192},{192,224},{1,3... | collective-permute-start | bytes 196616 | tf_op jit(solution)/shard_map/ppermute | solution.py:14
  173.7 0.4 fusion.73
  174.8 0.8 collective-permute-done.8
  175.6 1.4 maximum_bitcast_fusion.3
  177.0 10.1 %fusion.18 = (f32[18,128,128]{2,0,1:T(8,128)}, f32[18,128,128]{2,0,1:T(8,128)}, f32[18,128,128]{2,0,1:T(8,128)}, f32[18,128,128]{2,0,1:T(8,128)}, f32[18,128,128]{2,0,1:T(8,128)}, /*index=5*/f32[18,128,128]{2,0,1:T(8,128)}) fusion(f32[18,128,128]{2,0,1:T(8,128)} %maximum_bitcast_fusion.3), kind=kLoop, calls=%fused_computation.48 | loop fusion | flops 589824 | bytes 8257536 | tf_op jit(solution)/shard_map/sub | solution.py:32
  187.0 8.9 %fusion.70 = (f32[16,128,128]{2,0,1:T(8,128)}, f32[16,128,128]{2,0,1:T(8,128)}) fusion(f32[16,128,128]{2,0,1:T(8,128)S(1)} %fusion.37, f32[16,128,128]{2,0,1:T(8,128)} %copy-done.2, f32[16,128,128]{2,0,1:T(8,128)S(1)} %fusion.61, bf16[1,1,16,128,128]{4,3,2,1,0:T(8,128)(2,1)} %get-tuple-element.11, bf16[1,1,16,128,128]{4,3,2,1,0:T(8,128)(2,1)} %get-tuple-element.9, ...), kind=kLoop, calls=%fused_computation.133 | loop fusion | flops 8912896 | bytes 22085700 | tf_op jit(solution)/shard_map/mul | solution.py:91
  196.0 0.0 reduce-scatter.2.cloned.1.call-update
  196.0 1.3 copy.26
  197.3 1.3 copy.25
  198.6 125.7 %reduce-scatter.2.cloned.1.call-done = f32[16,4,128]{2,0,1:T(8,128)} async-done(((f32[16,128,128]{2,0,1:T(8,128)}), f32[16,4,128]{2,0,1:T(8,128)}) %reduce-scatter.2.cloned.1.call-update) | async-done | bytes 32784 | tf_op jit(solution)/shard_map/reduce_scatter | solution.py:92
  324.3 0.8 fusion.98
  325.1 0.6 copy.27
  (43 shorter events, 0.1 us)
Async XLA Ops:
  7.2 12.2 %copy-start.18 = (f32[16,4,128]{2,1,0:T(4,128)S(1)}, f32[16,4,128]{2,1,0:T(4,128)}, u32[]{:S(2)}) copy-start(f32[16,4,128]{2,1,0:T(4,128)} %param.13) | copy-start | bytes 98308
  7.2 12.9 %copy-start.5 = (f32[1,16,128,128]{3,2,1,0:T(8,128)S(1)}, f32[1,16,128,128]{3,2,1,0:T(8,128)}, u32[]{:S(2)}) copy-start(f32[1,16,128,128]{3,2,1,0:T(8,128)} %param.9) | copy-start | bytes 3145732
  9.2 39.3 %all-to-all-start = ((f32[32,16,4,128]{3,2,1,0:T(4,128)}), f32[32,16,4,128]{3,2,1,0:T(4,128)}, u32[]{:S(2)}, u32[]{:S(2)}) async-start(f32[32,16,4,128]{3,2,1,0:T(4,128)} %stack.8), calls=%async_computation | async-start | bytes 2097152 | tf_op jit(solution)/shard_map/all_to_all | solution.py:56
  19.2 8.3 %copy-start.19 = (f32[1,4,256]{2,1,0:T(4,128)S(1)}, f32[1,4,256]{2,1,0:T(4,128)}, u32[]{:S(2)}) copy-start(f32[1,4,256]{2,1,0:T(4,128)} %param.17) | copy-start | bytes 12292
  19.3 8.3 %copy-start.20 = (s32[1,256]{1,0:T(1,128)S(1)}, s32[1,256]{1,0:T(1,128)}, u32[]{:S(2)}) copy-start(s32[1,256]{1,0:T(1,128)} %param.16) | copy-start | bytes 3076
  19.3 8.3 %copy-start.21 = (s32[1,256]{1,0:T(1,128)S(1)}, s32[1,256]{1,0:T(1,128)}, u32[]{:S(2)}) copy-start(s32[1,256]{1,0:T(1,128)} %param.15) | copy-start | bytes 3076
  19.3 8.7 %copy-start.15 = (bf16[1,4,16,128,128]{4,3,2,1,0:T(8,128)(2,1)S(1)}, bf16[1,4,16,128,128]{4,3,2,1,0:T(8,128)(2,1)}, u32[]{:S(2)}) copy-start(bf16[1,4,16,128,128]{4,3,2,1,0:T(8,128)(2,1)} %param.11) | copy-start | bytes 6291460
  19.3 68.6 %all-gather.2.cloned.1.call-start = ((), (), s32[]{:S(2)}) async-start(), calls=%async_computation.2 | async-start | bytes 1081344 | tf_op jit(solution)/shard_map/all_gather | solution.py:65
  20.0 304.3 %reduce-scatter.2.cloned.1.call-start = ((), (), s32[]{:S(2)}) async-start(), calls=%async_computation.3 | async-start | bytes 1081344 | tf_op jit(solution)/shard_map/reduce_scatter | solution.py:92
  20.1 9.2 %collective-permute-start.3 = (f32[1,1,128,128]{3,1,2,0:T(1,128)S(1)}, f32[1,1,128,128]{3,1,2,0:T(1,128)S(1)}, u32[]{:S(2)}, u32[]{:S(2)}) collective-permute-start(f32[1,1,128,128]{3,1,2,0:T(1,128)S(1)} %bitcast.71), channel_id=1, source_target_pairs={{32,0},{64,32},{96,64},{128,96},{160,128},{192,160},{224,192},{33,... | collective-permute-start | bytes 196616 | tf_op jit(solution)/shard_map/ppermute | solution.py:15
  22.6 6.8 %collective-permute-start.2 = (f32[1,1,128,128]{3,1,2,0:T(1,128)S(1)}, f32[1,1,128,128]{3,1,2,0:T(1,128)S(1)}, u32[]{:S(2)}, u32[]{:S(2)}) collective-permute-start(f32[1,1,128,128]{3,1,2,0:T(1,128)S(1)} %bitcast.70), channel_id=1, source_target_pairs={{0,32},{32,64},{64,96},{96,128},{128,160},{160,192},{192,224},{1,3... | collective-permute-start | bytes 196616 | tf_op jit(solution)/shard_map/ppermute | solution.py:14
  28.0 1.8 copy-start.14
  30.1 65.6 %copy-start.3 = (f32[18,128,128]{2,0,1:T(8,128)}, f32[18,128,128]{2,0,1:T(8,128)S(1)}, u32[]{:S(2)}) copy-start(f32[18,128,128]{2,0,1:T(8,128)S(1)} %maximum_bitcast_fusion) | copy-start | bytes 3538948
  89.8 10.4 %collective-permute-start.1 = (f32[2,1,128,128]{3,1,2,0:T(1,128)S(1)}, f32[2,1,128,128]{3,1,2,0:T(1,128)S(1)}, u32[]{:S(2)}, u32[]{:S(2)}) collective-permute-start(f32[2,1,128,128]{3,1,2,0:T(1,128)S(1)} %get-tuple-element.13), channel_id=1, source_target_pairs={{32,0},{64,32},{96,64},{128,96},{160,128},{192,160},{224,192},{33,... | collective-permute-start | bytes 393224 | tf_op jit(solution)/shard_map/ppermute | solution.py:15
  92.2 8.0 %collective-permute-start = (f32[2,1,128,128]{3,1,2,0:T(1,128)S(1)}, f32[2,1,128,128]{3,1,2,0:T(1,128)S(1)}, u32[]{:S(2)}, u32[]{:S(2)}) collective-permute-start(f32[2,1,128,128]{3,1,2,0:T(1,128)S(1)} %get-tuple-element.12), channel_id=1, source_target_pairs={{0,32},{32,64},{64,96},{96,128},{128,160},{160,192},{192,224},{1,3... | collective-permute-start | bytes 393224 | tf_op jit(solution)/shard_map/ppermute | solution.py:14
  100.2 1.6 copy-start.12
  100.2 1.7 copy-start.16
  100.5 2.0 copy-start.4
  100.5 2.3 copy-start.6
  100.5 3.7 %copy-start.7 = (f32[18,128,128]{2,0,1:T(8,128)S(1)}, f32[18,128,128]{2,0,1:T(8,128)}, u32[]{:S(2)}) copy-start(f32[18,128,128]{2,0,1:T(8,128)} %get-tuple-element.38) | copy-start | bytes 3538948
  100.5 4.3 %copy-start.8 = (f32[18,128,128]{2,0,1:T(8,128)S(1)}, f32[18,128,128]{2,0,1:T(8,128)}, u32[]{:S(2)}) copy-start(f32[18,128,128]{2,0,1:T(8,128)} %get-tuple-element.39) | copy-start | bytes 3538948
  100.5 4.8 %copy-start.9 = (f32[18,128,128]{2,0,1:T(8,128)S(1)}, f32[18,128,128]{2,0,1:T(8,128)}, u32[]{:S(2)}) copy-start(f32[18,128,128]{2,0,1:T(8,128)} %get-tuple-element.40) | copy-start | bytes 3538948
  100.5 5.2 %copy-start.10 = (f32[18,128,128]{2,0,1:T(8,128)S(1)}, f32[18,128,128]{2,0,1:T(8,128)}, u32[]{:S(2)}) copy-start(f32[18,128,128]{2,0,1:T(8,128)} %get-tuple-element.41) | copy-start | bytes 3538948
  100.6 5.7 %copy-start.11 = (f32[18,128,128]{2,0,1:T(8,128)S(1)}, f32[18,128,128]{2,0,1:T(8,128)}, u32[]{:S(2)}) copy-start(f32[18,128,128]{2,0,1:T(8,128)} %get-tuple-element.42) | copy-start | bytes 3538948
  101.8 8.3 %copy-start = (f32[18,128,128]{2,0,1:T(8,128)}, f32[18,128,128]{2,0,1:T(8,128)S(1)}, u32[]{:S(2)}) copy-start(f32[18,128,128]{2,0,1:T(8,128)S(1)} %get-tuple-element.36) | copy-start | bytes 3538948
  101.9 8.3 %copy-start.1 = (f32[18,128,128]{2,0,1:T(8,128)}, f32[18,128,128]{2,0,1:T(8,128)S(1)}, u32[]{:S(2)}) copy-start(f32[18,128,128]{2,0,1:T(8,128)S(1)} %get-tuple-element.37) | copy-start | bytes 3538948
  110.3 6.3 %collective-permute-start.5 = (f32[1,1,128,128]{3,1,2,0:T(1,128)S(1)}, f32[1,1,128,128]{3,1,2,0:T(1,128)S(1)}, u32[]{:S(2)}, u32[]{:S(2)}) collective-permute-start(f32[1,1,128,128]{3,1,2,0:T(1,128)S(1)} %get-tuple-element.49), channel_id=1, source_target_pairs={{32,0},{64,32},{96,64},{128,96},{160,128},{192,160},{224,192},{33,... | collective-permute-start | bytes 196616 | tf_op jit(solution)/shard_map/ppermute | solution.py:15
  112.7 6.2 %collective-permute-start.4 = (f32[1,1,128,128]{3,1,2,0:T(1,128)S(1)}, f32[1,1,128,128]{3,1,2,0:T(1,128)S(1)}, u32[]{:S(2)}, u32[]{:S(2)}) collective-permute-start(f32[1,1,128,128]{3,1,2,0:T(1,128)S(1)} %get-tuple-element.48), channel_id=1, source_target_pairs={{0,32},{32,64},{64,96},{96,128},{128,160},{160,192},{192,224},{1,3... | collective-permute-start | bytes 196616 | tf_op jit(solution)/shard_map/ppermute | solution.py:14
  136.9 9.3 %copy-start.2 = (f32[16,128,128]{2,0,1:T(8,128)}, f32[16,128,128]{2,0,1:T(8,128)S(1)}, u32[]{:S(2)}) copy-start(f32[16,128,128]{2,0,1:T(8,128)S(1)} %fusion.49) | copy-start | bytes 3145732
  137.0 7.9 %collective-permute-start.7 = (f32[1,1,128,128]{3,1,2,0:T(1,128)S(1)}, f32[1,1,128,128]{3,1,2,0:T(1,128)S(1)}, u32[]{:S(2)}, u32[]{:S(2)}) collective-permute-start(f32[1,1,128,128]{3,1,2,0:T(1,128)S(1)} %get-tuple-element.47), channel_id=1, source_target_pairs={{32,0},{64,32},{96,64},{128,96},{160,128},{192,160},{224,192},{33,... | collective-permute-start | bytes 196616 | tf_op jit(solution)/shard_map/ppermute | solution.py:15
  138.9 7.2 %collective-permute-start.6 = (f32[1,1,128,128]{3,1,2,0:T(1,128)S(1)}, f32[1,1,128,128]{3,1,2,0:T(1,128)S(1)}, u32[]{:S(2)}, u32[]{:S(2)}) collective-permute-start(f32[1,1,128,128]{3,1,2,0:T(1,128)S(1)} %get-tuple-element.46), channel_id=1, source_target_pairs={{0,32},{32,64},{64,96},{96,128},{128,160},{160,192},{192,224},{1,3... | collective-permute-start | bytes 196616 | tf_op jit(solution)/shard_map/ppermute | solution.py:14
  164.2 10.5 %collective-permute-start.9 = (f32[1,1,128,128]{3,1,2,0:T(1,128)S(1)}, f32[1,1,128,128]{3,1,2,0:T(1,128)S(1)}, u32[]{:S(2)}, u32[]{:S(2)}) collective-permute-start(f32[1,1,128,128]{3,1,2,0:T(1,128)S(1)} %get-tuple-element.45), channel_id=1, source_target_pairs={{32,0},{64,32},{96,64},{128,96},{160,128},{192,160},{224,192},{33,... | collective-permute-start | bytes 196616 | tf_op jit(solution)/shard_map/ppermute | solution.py:15
  166.2 9.4 %collective-permute-start.8 = (f32[1,1,128,128]{3,1,2,0:T(1,128)S(1)}, f32[1,1,128,128]{3,1,2,0:T(1,128)S(1)}, u32[]{:S(2)}, u32[]{:S(2)}) collective-permute-start(f32[1,1,128,128]{3,1,2,0:T(1,128)S(1)} %get-tuple-element.44), channel_id=1, source_target_pairs={{0,32},{32,64},{64,96},{96,128},{128,160},{160,192},{192,224},{1,3... | collective-permute-start | bytes 196616 | tf_op jit(solution)/shard_map/ppermute | solution.py:14
  196.0 1.3 copy-start.13
  197.3 127.0 %copy-start.17 = (f32[16,4,128]{2,1,0:T(4,128)S(1)}, f32[16,4,128]{2,1,0:T(4,128)}, u32[]{:S(2)}) copy-start(f32[16,4,128]{2,1,0:T(4,128)} %param.12) | copy-start | bytes 98308
Sparse Core Ops, SparseCore 0:
  22.5 65.2 all-gather.1
  196.1 128.1 reduce-scatter.1
